TPU v7x, 128 devices: a whole 4x4x4 slice. The times are simulated.
128 devices in a mesh: section: 2 (over z_lo), cp: 16 (over y, z_hi, core), tp: 4 (over x).
Axes of the slice: x: 4, y: 4, z: 4 (z_hi: 2, z_lo: 2; z = z_hi * 2 + z_lo), core: 2. Of those that a mesh axis runs over, the one named last changes fastest.
Arguments:
- rollout_rows: bfloat16 [2048, 8192], P(('section', 'cp'), 'tp'), may hold values from -60 to 60
- lengths: int32 [2], replicated, may hold values from 1 to 1536, 2048 in all
- block_owner: int32 [32], replicated, may hold values from 0 to 31, each once
- norm_gain: float32 [2, 8192], P('section', 'tp'), may hold values from 0.1 to 1.9
- w_qkv: bfloat16 [2, 3, 8192, 8192], P('section', None, 'tp', 'cp'), may hold values from -1 to 1
- w_out: bfloat16 [2, 8192, 8192], P('section', 'cp', 'tp'), may hold values from -0.5 to 0.5
Outputs:
- scored: bfloat16 [2, 2048, 8192], P(None, ('section', 'cp'), 'tp')
Inputs may be any that keep to these rules, and one draw needn't show every extreme that they name: The 2 lengths sum to 2048; neither is over 1536. `block_owner`: every owner block appears once.
All inputs are finite; a program needn't handle non-finite values.
Results may differ from a plain program's by a relative error of at most 0.022.
Values may be sent and summed in bfloat16 or wider, within the bound.
No kernel may reach another device: no remote copies, remote signals or barrier semaphores. Data moves between devices by JAX's collectives and lax.ppermute only.
A program may use at most 128 MiB of HBM per device.

v0:
```python
import math
import jax
import jax.numpy as jnp
from jax import lax
from jax.sharding import PartitionSpec as P

D = 8192
HEAD = 128


def layout_position(layout_rows, tokens, tp_count):
    quarter = tokens // tp_count
    halfblock = quarter // 2
    owner_index = layout_rows // quarter
    second = layout_rows % quarter // halfblock
    offset = layout_rows % halfblock
    block_index = 2 * owner_index + second
    return block_index * halfblock + offset


def layout_row(position, tokens, tp_count):
    quarter = tokens // tp_count
    halfblock = quarter // 2
    block_index = position // halfblock
    offset = position % halfblock
    second = block_index % 2
    owner_index = block_index // 2
    return owner_index * quarter + second * halfblock + offset


def on_device(rollout_rows, lengths, block_owner, norm_gain, w_qkv, w_out):
    tp_count = lax.axis_size("tp")
    cp_count = lax.axis_size("cp")
    sections = lax.axis_size("section")
    own_rows, width_here = rollout_rows.shape
    blocks = sections * cp_count
    tokens = own_rows * blocks
    actor_rows = lax.all_gather(rollout_rows, ("section", "cp"), axis=0, tiled=True)
    layout_rows = jnp.arange(tokens, dtype=jnp.int32)
    position = layout_position(layout_rows, tokens, tp_count)
    source = block_owner[position // own_rows] * own_rows + position % own_rows
    rows_in = jnp.take(actor_rows, source, axis=0)
    seq_ends = jnp.cumsum(lengths)
    sequence = jnp.sum((position[:, None] >= seq_ends[None, :]).astype(jnp.int32), axis=1)
    squares = jnp.sum(jnp.square(rows_in.astype(jnp.float32)), axis=1)
    total_squares = lax.psum(squares, "tp")
    inverse_rms = lax.rsqrt(total_squares / D + 1e-05)
    normed = (rows_in.astype(jnp.float32) * norm_gain[0][None, :] * inverse_rms[:, None]).astype(
        jnp.bfloat16
    )
    qkv_weights = w_qkv[0]
    local_rows = tokens // tp_count
    halfblock = local_rows // 2
    heads_here = qkv_weights.shape[2] // HEAD
    first_local = lax.axis_index("tp") * local_rows
    query_pos = lax.dynamic_slice_in_dim(position, first_local, local_rows, 0).reshape(2, halfblock)
    query_seq = lax.dynamic_slice_in_dim(sequence, first_local, local_rows, 0).reshape(2, halfblock)
    inv_sqrt = 1.0 / math.sqrt(HEAD)
    initial = (
        jnp.full((2, heads_here, halfblock), -1e30, jnp.float32),
        jnp.zeros((2, heads_here, halfblock), jnp.float32),
        jnp.zeros((2, heads_here, halfblock, HEAD), jnp.float32),
    )
    projected = lax.psum_scatter(
        jnp.einsum("rd,kdc->rkc", normed, qkv_weights, preferred_element_type=jnp.float32),
        "tp",
        scatter_dimension=0,
        tiled=True,
    ).astype(jnp.bfloat16)
    query_blocks = projected[:, 0].reshape(2, halfblock, heads_here, HEAD)
    key_part = lax.all_gather(projected[:, 1], "tp", axis=0, tiled=True)
    value_part = lax.all_gather(projected[:, 2], "tp", axis=0, tiled=True)
    key_count = key_part.shape[0]
    key_heads = key_part.reshape(key_count, heads_here, HEAD)
    value_heads = value_part.reshape(key_count, heads_here, HEAD)
    results = []
    for sub_block in range(2):
        allowed = (query_seq[sub_block][:, None] == sequence[None, :]) & (
            position[None, :] <= query_pos[sub_block][:, None]
        )
        query_block = query_blocks[sub_block]

        def update(state_now):
            row_peak, row_total, weighted = state_now
            scores = (
                jnp.einsum(
                    "qhd,khd->hqk", query_block, key_heads, preferred_element_type=jnp.float32
                )
                * inv_sqrt
            )
            scores = jnp.where(allowed[None], scores, -1e30)
            new_peak = jnp.maximum(row_peak, jnp.max(scores, axis=2))
            weights_now = jnp.where(allowed[None], jnp.exp(scores - new_peak[:, :, None]), 0.0)
            row_total = jnp.sum(weights_now, axis=2)
            probabilities = weights_now.astype(jnp.bfloat16)
            weighted = jnp.einsum(
                "hqk,khd->hqd", probabilities, value_heads, preferred_element_type=jnp.float32
            )
            return (new_peak, row_total, weighted)

        def unchanged(state_now):
            return state_now

        results.append(
            lax.cond(
                jnp.any(allowed),
                update,
                unchanged,
                (initial[0][sub_block], initial[1][sub_block], initial[2][sub_block]),
            )
        )
    attended = (
        jnp.stack([results[0][2], results[1][2]])
        / jnp.stack([results[0][1], results[1][1]])[:, :, :, None]
    )
    attended = (
        attended.transpose(0, 2, 1, 3).reshape(local_rows, heads_here * HEAD).astype(jnp.bfloat16)
    )
    gathered = lax.all_gather(attended, "tp", axis=0, tiled=True)
    group_rows = sections * own_rows
    target_rows = jnp.arange(tokens, dtype=jnp.int32)
    cp_index = target_rows // group_rows
    owner_section = target_rows % group_rows // own_rows
    inner = target_rows % own_rows
    actor_block = owner_section * cp_count + cp_index
    block_ids = jnp.arange(blocks, dtype=jnp.int32)
    inverse_owner = jnp.sum(
        jnp.where(block_owner[None, :] == block_ids[:, None], block_ids[None, :], 0), axis=1
    )
    packed_pos = inverse_owner[actor_block] * own_rows + inner
    ordered = jnp.take(gathered, layout_row(packed_pos, tokens, tp_count), axis=0)
    out_weight = w_out[0]
    summed = lax.psum_scatter(
        jnp.dot(ordered, out_weight, preferred_element_type=jnp.float32).astype(jnp.bfloat16),
        "cp",
        scatter_dimension=0,
        tiled=True,
    )
    branch = summed.reshape(sections, own_rows, width_here)
    return lax.all_to_all(branch, "section", split_axis=0, concat_axis=0, tiled=True)


def solution(mesh):
    return jax.shard_map(
        on_device,
        mesh=mesh,
        in_specs=(
            P(("section", "cp"), "tp"),
            P(),
            P(),
            P("section", "tp"),
            P("section", None, "tp", "cp"),
            P("section", "cp", "tp"),
        ),
        out_specs=P(None, ("section", "cp"), "tp"),
        check_vma=False,
    )
```

profile of v0, /device:TPU:0, one launch (start us, length us, event | category | flops | bytes accessed | tf_op | source)
XLA Modules:
  0.0 519.2 jit_solution(15395411485198232677)
XLA Ops:
  14.3 4.6 compare_select_fusion.4
  18.9 15.4 %compare_and_fusion.2 = (pred[2048]{0:T(1024)(128)(4,1)S(1)}, s32[2048]{0:T(1024)S(1)}) fusion(pred[2048]{0:T(1024)(128)(4,1)S(1)} %compare_reduce_fusion, pred[2048]{0:T(1024)(128)(4,1)S(1)} %compare_reduce_fusion.1, pred[2048]{0:T(1024)(128)(4,1)S(1)} %compare_reduce_fusion.2, pred[2048]{0:T(1024)(128)(4,1)S(1)} %compare_reduce_fusion.3, ...), kind=kLoop, calls=%fused_computation.236 | loop fusion | flops 165888 | bytes 69732 | tf_op jit(solution)/shard_map/jit(_take)/and | solution.py:42
  34.4 43.7 %all-gather.7.cloned.1.call-done = bf16[2048,2048]{1,0:T(8,128)(2,1)} async-done(((bf16[64,2048]{1,0:T(8,128)(2,1)}), bf16[2048,2048]{1,0:T(8,128)(2,1)}) %all-gather.7.cloned.1.call-update) | async-done | bytes 8388624 | tf_op jit(solution)/shard_map/all_gather | solution.py:38
  78.0 20.8 %gather_fusion = bf16[2048,2048]{1,0:T(8,128)(2,1)} fusion(bf16[2048,2048]{1,0:T(8,128)(2,1)} %all-gather.7.cloned.1.call-done, s32[2048]{0:T(1024)S(1)} %broadcast_clamp_fusion.1), kind=kCustom, calls=%fused_computation | custom fusion | bytes 16785408 | tf_op jit(solution)/shard_map/jit(_take)/gather | solution.py:42
  98.8 5.7 %fusion.36 = f32[2048]{0:T(1024)S(1)} fusion(bf16[2048,2048]{1,0:T(8,128)(2,1)} %gather_fusion, pred[2048]{0:T(1024)(128)(4,1)S(1)} %get-tuple-element.73), kind=kLoop, calls=%fused_computation.36 | loop fusion | flops 16775168 | bytes 8398848 | tf_op jit(solution)/shard_map/reduce_sum | solution.py:45
  104.6 10.7 %psum.7 = f32[2048]{0:T(1024)S(1)} all-reduce(f32[2048]{0:T(1024)S(1)} %fusion.36), channel_id=1, replica_groups=mesh['section'=2,'cp'=16,'tp'=4] {'tp'}, use_global_device_ids=true, to_apply=%region_5.6 | all-reduce | flops 2048 | bytes 16384 | tf_op jit(solution)/shard_map/psum | solution.py:46
  115.3 20.0 %fusion.38 = f32[2048,3,512]{2,0,1:T(8,128)} fusion(f32[2048]{0:T(1024)S(1)} %add_rsqrt_fusion, f32[2048]{0:T(1024)S(1)} %bitcast.118, bf16[1,3,2048,512]{3,2,1,0:T(8,128)(2,1)} %param.14, bf16[2048,2048]{1,0:T(8,128)(2,1)} %gather_fusion, pred[2048]{0:T(1024)(128)(4,1)S(1)} %get-tuple-element.73), kind=kOutput, calls=%fused_computation.38 | convolution fusion | flops 12905873408 | bytes 27281408 | tf_op jit(solution)/shard_map/rd,kdc->rkc/dot_general | solution.py:65
  135.4 111.7 %reduce-scatter.3.cloned.1.call-done = f32[512,3,512]{2,0,1:T(8,128)} async-done(((f32[2048,3,512]{2,0,1:T(8,128)}), f32[512,3,512]{2,0,1:T(8,128)}) %reduce-scatter.3.cloned.1.call-update) | async-done | bytes 3145744 | tf_op jit(solution)/shard_map/reduce_scatter | solution.py:64
  255.7 26.5 %all-gather.11.cloned.1.call-done = bf16[2048,1,512]{2,0,1:T(8,128)(2,1)} async-done(((bf16[512,1,512]{2,0,1:T(8,128)(2,1)}), bf16[2048,1,512]{2,0,1:T(8,128)(2,1)}) %all-gather.11.cloned.1.call-update) | async-done | bytes 2097168 | tf_op jit(solution)/shard_map/all_gather | solution.py:71
  282.2 4.0 reshape.639
  286.2 28.4 %all-gather.13.cloned.1.call-done = bf16[2048,1,512]{2,0,1:T(8,128)(2,1)} async-done(((bf16[512,1,512]{2,0,1:T(8,128)(2,1)}), bf16[2048,1,512]{2,0,1:T(8,128)(2,1)}) %all-gather.13.cloned.1.call-update) | async-done | bytes 2097168 | tf_op jit(solution)/shard_map/all_gather | solution.py:72
  314.6 4.0 reshape.640
  318.6 13.3 %conditional.2 = (f32[1,4,256]{2,1,0:T(4,128)S(1)}, f32[1,4,256,128]{3,2,1,0:T(8,128)}) conditional(s32[]{:T(128)} %convert_element_type.38, () %tuple.29, (pred[256,2048]{1,0:T(8,128)(4,1)S(1)}, bf16[512,3,512]{2,0,1:T(8,128)(2,1)}, bf16[2048,4,128]{2,1,0:T(4,128)(2,1)}, bf16[2048,4,128]{2,1,0:T(4,128)(2,1)}) %tuple.128), branch_computations={%region_7.8_spmd, %region_8.11_spmd} | conditional | flops 1101003776 | bytes 43802668 | solution.py:105
  322.3 3.7 fusion
  326.0 3.4 fusion.9
  331.9 12.8 %conditional.3 = (f32[1,4,256]{2,1,0:T(4,128)S(1)}, f32[1,4,256,128]{3,2,1,0:T(8,128)S(1)}) conditional(s32[]{:T(128)} %convert_element_type.42, () %tuple.31, (pred[256,2048]{1,0:T(8,128)(4,1)S(1)}, bf16[512,3,512]{2,0,1:T(8,128)(2,1)}, bf16[2048,4,128]{2,1,0:T(4,128)(2,1)}, bf16[2048,4,128]{2,1,0:T(4,128)(2,1)}) %tuple.129), branch_computations={%region_12.13_spmd, %region_13.16_spmd} | conditional | flops 1101003776 | bytes 43802668 | solution.py:105
  335.9 3.7 fusion.17
  351.7 4.6 compare_select_fusion.10
  356.3 15.4 %compare_and_fusion.3 = (pred[2048]{0:T(1024)(128)(4,1)S(1)}, s32[2048]{0:T(1024)S(1)}) fusion(pred[2048]{0:T(1024)(128)(4,1)S(1)} %compare_reduce_fusion.25, pred[2048]{0:T(1024)(128)(4,1)S(1)} %compare_reduce_fusion.26, pred[2048]{0:T(1024)(128)(4,1)S(1)} %compare_reduce_fusion.27, pred[2048]{0:T(1024)(128)(4,1)S(1)} %compare_reduce_fusion.28, ...), kind=kLoop, calls=%fused_computation.237 | loop fusion | flops 165888 | bytes 69732 | tf_op jit(solution)/shard_map/jit(_take)/and | solution.py:131
  371.9 6.6 %all-gather.9.cloned.1.call-done = bf16[2048,512]{1,0:T(8,128)(2,1)} async-done(((bf16[512,512]{1,0:T(8,128)(2,1)}), bf16[2048,512]{1,0:T(8,128)(2,1)}) %all-gather.9.cloned.1.call-update) | async-done | bytes 2097168 | tf_op jit(solution)/shard_map/all_gather | solution.py:119
  378.5 11.1 %gather_fusion.1 = bf16[2048,512]{1,0:T(8,128)(2,1)} fusion(bf16[2048,512]{1,0:T(8,128)(2,1)} %all-gather.9.cloned.1.call-done, s32[2048]{0:T(1024)S(1)} %broadcast_clamp_fusion), kind=kCustom, calls=%fused_computation.1 | custom fusion | bytes 4202496 | tf_op jit(solution)/shard_map/jit(_take)/gather | solution.py:131
  389.5 8.5 %convolution_convert_fusion = bf16[2048,2048]{1,0:T(8,128)(2,1)} fusion(bf16[1,512,2048]{2,1,0:T(8,128)(2,1)S(1)} %copy-done, bf16[2048,512]{1,0:T(8,128)(2,1)} %gather_fusion.1, pred[2048]{0:T(1024)(128)(4,1)S(1)} %get-tuple-element.69), kind=kOutput, calls=%fused_computation.42 | convolution fusion | flops 4300210176 | bytes 12584960 | tf_op jit(solution)/shard_map/dot_general | solution.py:134
  398.0 102.8 %reduce-scatter.5.cloned.1.call-done = bf16[128,2048]{1,0:T(8,128)(2,1)} async-done(((bf16[2048,2048]{1,0:T(8,128)(2,1)}), bf16[128,2048]{1,0:T(8,128)(2,1)}) %reduce-scatter.5.cloned.1.call-update) | async-done | bytes 524304 | tf_op jit(solution)/shard_map/reduce_scatter | solution.py:133
  500.8 10.7 %all_to_all.5 = bf16[2,64,2048]{2,1,0:T(8,128)(2,1)S(1)} all-to-all(bf16[2,64,2048]{2,1,0:T(8,128)(2,1)} %bitcast.108), channel_id=1, replica_groups=mesh['section'=2,'cp'=16,'tp'=4] {'section'}, dimensions={0} | all-to-all | bytes 1048576 | tf_op jit(solution)/shard_map/all_to_all | solution.py:140
  (109 shorter events, 38.0 us)
Async XLA Ops:
  6.5 383.0 %copy-start = (bf16[1,512,2048]{2,1,0:T(8,128)(2,1)S(1)}, bf16[1,512,2048]{2,1,0:T(8,128)(2,1)}, u32[]{:S(2)}) copy-start(bf16[1,512,2048]{2,1,0:T(8,128)(2,1)} %param.15) | copy-start | bytes 6291460
  6.5 71.5 %all-gather.7.cloned.1.call-start = ((), (), s32[]{:S(2)}) async-start(), calls=%async_computation.3 | async-start | bytes 8650752 | tf_op jit(solution)/shard_map/all_gather | solution.py:38
  7.3 239.9 %reduce-scatter.3.cloned.1.call-start = ((), (), s32[]{:S(2)}) async-start(), calls=%async_computation.4 | async-start | bytes 15728640 | tf_op jit(solution)/shard_map/reduce_scatter | solution.py:64
  98.8 16.5 %copy-start.5 = (f32[1,2048]{1,0:T(1,128)S(1)}, f32[1,2048]{1,0:T(1,128)}, u32[]{:S(2)}) copy-start(f32[1,2048]{1,0:T(1,128)} %param.13) | copy-start | bytes 24580
  135.4 116.9 %copy-start.6 = (s32[2]{0:T(128)S(1)}, s32[2]{0:T(128)}, u32[]{:S(2)}) copy-start(s32[2]{0:T(128)} %param.11) | copy-start | bytes 28
  135.4 146.8 %all-gather.11.cloned.1.call-start = ((), (), s32[]{:S(2)}) async-start(), calls=%async_computation.7 | async-start | bytes 2621440 | tf_op jit(solution)/shard_map/all_gather | solution.py:71
  249.3 1.1 copy-start.1
  251.5 63.1 %all-gather.13.cloned.1.call-start = ((), (), s32[]{:S(2)}) async-start(), calls=%async_computation.8 | async-start | bytes 2621440 | tf_op jit(solution)/shard_map/all_gather | solution.py:72
  252.1 126.4 %all-gather.9.cloned.1.call-start = ((), (), s32[]{:S(2)}) async-start(), calls=%async_computation.5 | async-start | bytes 2621440 | tf_op jit(solution)/shard_map/all_gather | solution.py:119
  321.1 4.8 copy-start.2
  331.9 18.2 %copy-start.4 = (s32[32]{0:T(128)S(1)}, s32[32]{0:T(128)}, u32[]{:S(2)}) copy-start(s32[32]{0:T(128)} %param.12) | copy-start | bytes 388
  334.8 4.8 copy-start.3
  347.5 153.4 %reduce-scatter.5.cloned.1.call-start = ((), (), s32[]{:S(2)}) async-start(), calls=%async_computation.6 | async-start | bytes 8912896 | tf_op jit(solution)/shard_map/reduce_scatter | solution.py:133
Sparse Core Ops, SparseCore 0:
  9.1 68.9 all-gather.6
  135.5 111.6 reduce-scatter.2
  251.6 30.5 all-gather.10
  283.7 30.8 all-gather.12
  347.6 30.8 all-gather.8
  398.1 102.6 reduce-scatter.4
where the time goes:
time: 521 us; the launch traced here: 519 us
  waiting for transfers between devices  321 us (62%)
  other arithmetic  62.2 us (12%)
  local copies, waits for them, and re-layouts  57 us (11%)
  matrix products  42 us (8%)
  blocking collectives  21.5 us (4%)
  between operations  14.9 us (3%)
    reduce_scatter x1, waiting for transfers between devices, on_device(): lax.psum_scatter(jnp.einsum('rd,kdc->rkc', normed, qkv_weights, preferred...  112 us
    reduce_scatter x1, waiting for transfers between devices, on_device(): lax.psum_scatter(jnp.dot(ordered, out_weight, preferred_element_type=jnp....  103 us
    all_gather x1, waiting for transfers between devices, on_device(): lax.all_gather(rollout_rows, ('section', 'cp'), axis=0, tiled=True)  43.7 us
    all_gather x1, waiting for transfers between devices, on_device(): value_part = lax.all_gather(projected[:, 2], 'tp', axis=0, tiled=True)  28.4 us
    all_gather x1, waiting for transfers between devices, on_device(): key_part = lax.all_gather(projected[:, 1], 'tp', axis=0, tiled=True)  26.5 us
    gather x1, local copies, waits for them, and re-layouts, on_device(): rows_in = jnp.take(actor_rows, source, axis=0)  20.8 us
    dot_general x1, matrix products, on_device(): jnp.einsum('rd,kdc->rkc', normed, qkv_weights, preferred_element_type=jnp...  20 us
    and x1, other arithmetic, on_device(): jnp.take(gathered, layout_row(packed_pos, tokens, tp_count), axis=0)  15.4 us
  transfers between devices with their start and end apart: 6, of which 6 were waited for; matrix products, arithmetic and copies ran while one was open for 11% of the time, Pallas kernels for 0%

commit v1 on v0

--- a/solution.py
+++ b/solution.py
@@ -29,6 +29,22 @@
 
 
 def on_device(rollout_rows, lengths, block_owner, norm_gain, w_qkv, w_out):
+
+    def _pack_regions(matrix, d0):
+        axis_tag = "tp"
+        wide_n = jax.lax.axis_size(axis_tag)
+        tray = [(at, (at + 1) % wide_n) for at in range(wide_n)]
+        block_list = [(at, (at - 1) % wide_n) for at in range(wide_n)]
+        response, high = ([matrix], [matrix])
+        for _ in range(wide_n // 2):
+            response.append(jax.lax.ppermute(response[-1], axis_tag, tray))
+        for _ in range((wide_n - 1) // 2):
+            high.append(jax.lax.ppermute(high[-1], axis_tag, block_list))
+        x_next = jnp.concatenate([*response[::-1], *high[1:]], axis=d0)
+        return jnp.roll(
+            x_next, shift=(jax.lax.axis_index(axis_tag) - wide_n // 2) * matrix.shape[d0], axis=d0
+        )
+
     tp_count = lax.axis_size("tp")
     cp_count = lax.axis_size("cp")
     sections = lax.axis_size("section")
@@ -69,7 +85,7 @@
     ).astype(jnp.bfloat16)
     query_blocks = projected[:, 0].reshape(2, halfblock, heads_here, HEAD)
     key_part = lax.all_gather(projected[:, 1], "tp", axis=0, tiled=True)
-    value_part = lax.all_gather(projected[:, 2], "tp", axis=0, tiled=True)
+    value_part = _pack_regions(projected[:, 2], d0=0)
     key_count = key_part.shape[0]
     key_heads = key_part.reshape(key_count, heads_here, HEAD)
     value_heads = value_part.reshape(key_count, heads_here, HEAD)

time: 521 us -> 513 us (0.985)
  waiting for transfers between devices: 321 us -> 301 us
  local copies, waits for them, and re-layouts: 57 us -> 67.1 us
    ppermute x0 -> x3, waiting for transfers between devices: none -> 36.6 us  [the longest x2 36.6 us: _pack_regions(): response.append(jax.lax.ppermute(response[-1], axis_tag, tray))]
    all_gather x1 -> x0, waiting for transfers between devices: 28.4 us -> none  [on_device(): value_part = lax.all_gather(projected[:, 2], 'tp', axis=0, tiled=True)]
    all_gather x1, waiting for transfers between devices: 26.5 us -> 0.01 us  [on_device(): key_part = lax.all_gather(projected[:, 1], 'tp', axis=0, tiled=True)]
    unnamed x12 -> x19, local copies, waits for them, and re-layouts: 2.82 us -> 10.4 us
    dynamic_slice x0 -> x2, local copies, waits for them, and re-layouts: none -> 5.44 us  [_pack_regions(): jnp.roll(x_next, shift=(jax.lax.axis_index(axis_tag) - wide_n // 2) * mat...]
  transfers between devices with their start and end apart: 6 -> 8, of which waited for: 6 -> 6; matrix products, arithmetic and copies ran while one was open for 11% -> 13% of each run, Pallas kernels for 0% -> 0%
where the time goes in v1:
time: 513 us; the launch traced here: 511 us
  waiting for transfers between devices  301 us (59%)
  local copies, waits for them, and re-layouts  67.1 us (13%)
  other arithmetic  62.1 us (12%)
  matrix products  41.1 us (8%)
  blocking collectives  21.2 us (4%)
  between operations  14.5 us (3%)
    reduce_scatter x1, waiting for transfers between devices, on_device(): lax.psum_scatter(jnp.einsum('rd,kdc->rkc', normed, qkv_weights, preferred...  112 us
    reduce_scatter x1, waiting for transfers between devices, on_device(): lax.psum_scatter(jnp.dot(ordered, out_weight, preferred_element_type=jnp....  103 us
    all_gather x1, waiting for transfers between devices, on_device(): lax.all_gather(rollout_rows, ('section', 'cp'), axis=0, tiled=True)  43.7 us
    ppermute x2, waiting for transfers between devices, _pack_regions(): response.append(jax.lax.ppermute(response[-1], axis_tag, tray))  36.6 us
    gather x1, local copies, waits for them, and re-layouts, on_device(): rows_in = jnp.take(actor_rows, source, axis=0)  20.8 us
    dot_general x1, matrix products, on_device(): jnp.einsum('rd,kdc->rkc', normed, qkv_weights, preferred_element_type=jnp...  20 us
    and x1, other arithmetic, on_device(): jnp.take(gathered, layout_row(packed_pos, tokens, tp_count), axis=0)  15.4 us
    and x1, other arithmetic, on_device(): rows_in = jnp.take(actor_rows, source, axis=0)  15.4 us
  transfers between devices with their start and end apart: 8, of which 6 were waited for; matrix products, arithmetic and copies ran while one was open for 13% of the time, Pallas kernels for 0%

profile of v1, /device:TPU:0, one launch (start us, length us, event | category | flops | bytes accessed | tf_op | source)
XLA Modules:
  0.0 511.1 jit_solution(6483839448546189876)
XLA Ops:
  14.3 4.6 compare_select_fusion.4
  18.9 15.4 %compare_and_fusion.2 = (pred[2048]{0:T(1024)(128)(4,1)S(1)}, s32[2048]{0:T(1024)S(1)}) fusion(pred[2048]{0:T(1024)(128)(4,1)S(1)} %compare_reduce_fusion, pred[2048]{0:T(1024)(128)(4,1)S(1)} %compare_reduce_fusion.1, pred[2048]{0:T(1024)(128)(4,1)S(1)} %compare_reduce_fusion.2, pred[2048]{0:T(1024)(128)(4,1)S(1)} %compare_reduce_fusion.3, ...), kind=kLoop, calls=%fused_computation.243 | loop fusion | flops 165888 | bytes 69732 | tf_op jit(solution)/shard_map/jit(_take)/and | solution.py:58
  34.4 43.7 %all-gather.5.cloned.1.call-done = bf16[2048,2048]{1,0:T(8,128)(2,1)} async-done(((bf16[64,2048]{1,0:T(8,128)(2,1)}), bf16[2048,2048]{1,0:T(8,128)(2,1)}) %all-gather.5.cloned.1.call-update) | async-done | bytes 8388624 | tf_op jit(solution)/shard_map/all_gather | solution.py:54
  78.0 20.8 %gather_fusion = bf16[2048,2048]{1,0:T(8,128)(2,1)} fusion(bf16[2048,2048]{1,0:T(8,128)(2,1)} %all-gather.5.cloned.1.call-done, s32[2048]{0:T(1024)S(1)} %broadcast_clamp_fusion.1), kind=kCustom, calls=%fused_computation | custom fusion | bytes 16785408 | tf_op jit(solution)/shard_map/jit(_take)/gather | solution.py:58
  98.8 5.7 %fusion.30 = f32[2048]{0:T(1024)S(1)} fusion(bf16[2048,2048]{1,0:T(8,128)(2,1)} %gather_fusion, pred[2048]{0:T(1024)(128)(4,1)S(1)} %get-tuple-element.73), kind=kLoop, calls=%fused_computation.34 | loop fusion | flops 16775168 | bytes 8398848 | tf_op jit(solution)/shard_map/reduce_sum | solution.py:61
  104.6 10.7 %psum.7 = f32[2048]{0:T(1024)S(1)} all-reduce(f32[2048]{0:T(1024)S(1)} %fusion.30), channel_id=1, replica_groups=mesh['section'=2,'cp'=16,'tp'=4] {'tp'}, use_global_device_ids=true, to_apply=%region_5.6 | all-reduce | flops 2048 | bytes 16384 | tf_op jit(solution)/shard_map/psum | solution.py:62
  115.3 20.0 %fusion.32 = f32[2048,3,512]{2,0,1:T(8,128)} fusion(f32[2048]{0:T(1024)S(1)} %add_rsqrt_fusion, f32[2048]{0:T(1024)S(1)} %bitcast.127, bf16[1,3,2048,512]{3,2,1,0:T(8,128)(2,1)} %param.14, bf16[2048,2048]{1,0:T(8,128)(2,1)} %gather_fusion, pred[2048]{0:T(1024)(128)(4,1)S(1)} %get-tuple-element.73), kind=kOutput, calls=%fused_computation.36 | convolution fusion | flops 12905873408 | bytes 27281408 | tf_op jit(solution)/shard_map/rd,kdc->rkc/dot_general | solution.py:81
  135.5 111.7 %reduce-scatter.3.cloned.1.call-done = f32[512,3,512]{2,0,1:T(8,128)} async-done(((f32[2048,3,512]{2,0,1:T(8,128)}), f32[512,3,512]{2,0,1:T(8,128)}) %reduce-scatter.3.cloned.1.call-update) | async-done | bytes 3145744 | tf_op jit(solution)/shard_map/reduce_scatter | solution.py:80
  252.3 17.3 %collective-permute-done = bf16[512,512]{1,0:T(8,128)(2,1)} collective-permute-done((bf16[512,512]{1,0:T(8,128)(2,1)}, bf16[512,512]{1,0:T(8,128)(2,1)}, u32[]{:S(2)}, u32[]{:S(2)}) %collective-permute-start) | collective-permute-done | bytes 524320 | tf_op jit(solution)/shard_map/ppermute | solution.py:40
  269.6 3.2 collective-permute-start.2
  275.6 19.3 %collective-permute-done.1 = bf16[512,512]{1,0:T(8,128)(2,1)} collective-permute-done((bf16[512,512]{1,0:T(8,128)(2,1)}, bf16[512,512]{1,0:T(8,128)(2,1)}, u32[]{:S(2)}, u32[]{:S(2)}) %collective-permute-start.1) | collective-permute-done | bytes 524320 | tf_op jit(solution)/shard_map/ppermute | solution.py:40
  305.1 4.0 copy.24
  309.0 4.0 reshape.639
  313.0 12.9 %conditional.2 = (f32[1,4,256]{2,1,0:T(4,128)S(1)}, f32[1,4,256,128]{3,2,1,0:T(8,128)}) conditional(s32[]{:T(128)} %convert_element_type.38, () %tuple.29, (pred[256,2048]{1,0:T(8,128)(4,1)S(1)}, bf16[512,3,512]{2,0,1:T(8,128)(2,1)}, bf16[2048,4,128]{2,1,0:T(4,128)(2,1)}, bf16[2048,4,128]{0,2,1:T(8,128)(2,1)}) %tuple.128), branch_computations={%region_7.8_spmd, %region_8.11_spmd} | conditional | flops 1101003776 | bytes 43802668 | solution.py:121
  316.7 3.7 fusion
  326.0 12.4 %conditional.3 = (f32[1,4,256]{2,1,0:T(4,128)S(1)}, f32[1,4,256,128]{3,2,1,0:T(8,128)S(1)}) conditional(s32[]{:T(128)} %convert_element_type.42, () %tuple.31, (pred[256,2048]{1,0:T(8,128)(4,1)S(1)}, bf16[512,3,512]{2,0,1:T(8,128)(2,1)}, bf16[2048,4,128]{2,1,0:T(4,128)(2,1)}, bf16[2048,4,128]{0,2,1:T(8,128)(2,1)}) %tuple.129), branch_computations={%region_12.13_spmd, %region_13.16_spmd} | conditional | flops 1101003776 | bytes 43802668 | solution.py:121
  329.9 3.7 fusion.14
  345.3 4.6 compare_select_fusion.10
  349.9 15.4 %compare_and_fusion.3 = (pred[2048]{0:T(1024)(128)(4,1)S(1)}, s32[2048]{0:T(1024)S(1)}) fusion(pred[2048]{0:T(1024)(128)(4,1)S(1)} %compare_reduce_fusion.25, pred[2048]{0:T(1024)(128)(4,1)S(1)} %compare_reduce_fusion.26, pred[2048]{0:T(1024)(128)(4,1)S(1)} %compare_reduce_fusion.27, pred[2048]{0:T(1024)(128)(4,1)S(1)} %compare_reduce_fusion.28, ...), kind=kLoop, calls=%fused_computation.244 | loop fusion | flops 165888 | bytes 69732 | tf_op jit(solution)/shard_map/jit(_take)/and | solution.py:147
  365.5 5.4 %all-gather.7.cloned.1.call-done = bf16[2048,512]{1,0:T(8,128)(2,1)} async-done(((bf16[512,512]{1,0:T(8,128)(2,1)}), bf16[2048,512]{1,0:T(8,128)(2,1)}) %all-gather.7.cloned.1.call-update) | async-done | bytes 2097168 | tf_op jit(solution)/shard_map/all_gather | solution.py:135
  370.9 11.1 %gather_fusion.1 = bf16[2048,512]{1,0:T(8,128)(2,1)} fusion(bf16[2048,512]{1,0:T(8,128)(2,1)} %all-gather.7.cloned.1.call-done, s32[2048]{0:T(1024)S(1)} %broadcast_clamp_fusion), kind=kCustom, calls=%fused_computation.1 | custom fusion | bytes 4202496 | tf_op jit(solution)/shard_map/jit(_take)/gather | solution.py:147
  382.0 8.5 %convolution_convert_fusion = bf16[2048,2048]{1,0:T(8,128)(2,1)} fusion(bf16[1,512,2048]{2,1,0:T(8,128)(2,1)S(1)} %copy-done, bf16[2048,512]{1,0:T(8,128)(2,1)} %gather_fusion.1, pred[2048]{0:T(1024)(128)(4,1)S(1)} %get-tuple-element.69), kind=kOutput, calls=%fused_computation.40 | convolution fusion | flops 4300210176 | bytes 12584960 | tf_op jit(solution)/shard_map/dot_general | solution.py:150
  390.5 102.8 %reduce-scatter.5.cloned.1.call-done = bf16[128,2048]{1,0:T(8,128)(2,1)} async-done(((bf16[2048,2048]{1,0:T(8,128)(2,1)}), bf16[128,2048]{1,0:T(8,128)(2,1)}) %reduce-scatter.5.cloned.1.call-update) | async-done | bytes 524304 | tf_op jit(solution)/shard_map/reduce_scatter | solution.py:149
  493.3 10.5 %all_to_all.5 = bf16[2,64,2048]{2,1,0:T(8,128)(2,1)S(1)} all-to-all(bf16[2,64,2048]{2,1,0:T(8,128)(2,1)} %bitcast.117), channel_id=1, replica_groups=mesh['section'=2,'cp'=16,'tp'=4] {'section'}, dimensions={0} | all-to-all | bytes 1048576 | tf_op jit(solution)/shard_map/all_to_all | solution.py:156
  (121 shorter events, 50.2 us)
Async XLA Ops:
  6.5 375.4 %copy-start = (bf16[1,512,2048]{2,1,0:T(8,128)(2,1)S(1)}, bf16[1,512,2048]{2,1,0:T(8,128)(2,1)}, u32[]{:S(2)}) copy-start(bf16[1,512,2048]{2,1,0:T(8,128)(2,1)} %param.15) | copy-start | bytes 6291460
  6.5 71.5 %all-gather.5.cloned.1.call-start = ((), (), s32[]{:S(2)}) async-start(), calls=%async_computation.3 | async-start | bytes 8650752 | tf_op jit(solution)/shard_map/all_gather | solution.py:54
  7.3 239.9 %reduce-scatter.3.cloned.1.call-start = ((), (), s32[]{:S(2)}) async-start(), calls=%async_computation.4 | async-start | bytes 15728640 | tf_op jit(solution)/shard_map/reduce_scatter | solution.py:80
  98.8 16.5 %copy-start.5 = (f32[1,2048]{1,0:T(1,128)S(1)}, f32[1,2048]{1,0:T(1,128)}, u32[]{:S(2)}) copy-start(f32[1,2048]{1,0:T(1,128)} %param.13) | copy-start | bytes 24580
  135.4 116.5 %copy-start.6 = (s32[2]{0:T(128)S(1)}, s32[2]{0:T(128)}, u32[]{:S(2)}) copy-start(s32[2]{0:T(128)} %param.11) | copy-start | bytes 28
  135.4 173.6 %all-gather.9.cloned.1.call-start = ((), (), s32[]{:S(2)}) async-start(), calls=%async_computation.7 | async-start | bytes 2621440 | tf_op jit(solution)/shard_map/all_gather | solution.py:87
  249.3 1.1 copy-start.1
  251.5 119.4 %all-gather.7.cloned.1.call-start = ((), (), s32[]{:S(2)}) async-start(), calls=%async_computation.5 | async-start | bytes 2621440 | tf_op jit(solution)/shard_map/all_gather | solution.py:135
  251.5 18.1 %collective-permute-start = (bf16[512,512]{1,0:T(8,128)(2,1)}, bf16[512,512]{1,0:T(8,128)(2,1)}, u32[]{:S(2)}, u32[]{:S(2)}) collective-permute-start(bf16[512,512]{1,0:T(8,128)(2,1)} %get-tuple-element.81), channel_id=1, source_target_pairs={{0,1},{1,2},{2,3},{3,0},{4,5},{5,6},{6,7},{7,4},{8,9},{9,10},{10,1... | collective-permute-start | bytes 1572872 | tf_op jit(solution)/shard_map/ppermute | solution.py:40
  269.6 25.3 %collective-permute-start.1 = (bf16[512,512]{1,0:T(8,128)(2,1)}, bf16[512,512]{1,0:T(8,128)(2,1)}, u32[]{:S(2)}, u32[]{:S(2)}) collective-permute-start(bf16[512,512]{1,0:T(8,128)(2,1)} %collective-permute-done), channel_id=1, source_target_pairs={{0,1},{1,2},{2,3},{3,0},{4,5},{5,6},{6,7},{7,4},{8,9},{9,10},{10,1... | collective-permute-start | bytes 1572872 | tf_op jit(solution)/shard_map/ppermute | solution.py:40
  269.6 28.6 %collective-permute-start.2 = (bf16[512,512]{1,0:T(8,128)(2,1)}, bf16[512,512]{1,0:T(8,128)(2,1)}, u32[]{:S(2)}, u32[]{:S(2)}) collective-permute-start(bf16[512,512]{1,0:T(8,128)(2,1)} %get-tuple-element.81), channel_id=1, source_target_pairs={{0,3},{1,0},{2,1},{3,2},{4,7},{5,4},{6,5},{7,6},{8,11},{9,8},{10,9... | collective-permute-start | bytes 1572872 | tf_op jit(solution)/shard_map/ppermute | solution.py:42
  315.6 4.8 copy-start.2
  325.9 17.8 %copy-start.4 = (s32[32]{0:T(128)S(1)}, s32[32]{0:T(128)}, u32[]{:S(2)}) copy-start(s32[32]{0:T(128)} %param.12) | copy-start | bytes 388
  328.8 4.8 copy-start.3
  341.1 152.2 %reduce-scatter.5.cloned.1.call-start = ((), (), s32[]{:S(2)}) async-start(), calls=%async_computation.6 | async-start | bytes 8912896 | tf_op jit(solution)/shard_map/reduce_scatter | solution.py:149
Sparse Core Ops, SparseCore 0:
  9.1 68.9 all-gather.4
  135.5 111.6 reduce-scatter.2
  251.6 43.1 all-gather.8
  341.2 29.6 all-gather.6
  390.6 102.6 reduce-scatter.4
